TPU v7x, 256 devices: a whole 4x4x8 slice. The times are simulated.
256 devices in a mesh: row: 2 (over core), col: 2 (over x_lo), rhs: 64 (over z, y, x_hi).
Axes of the slice: x: 4 (x_hi: 2, x_lo: 2; x = x_hi * 2 + x_lo), y: 4, z: 8, core: 2. Of those that a mesh axis runs over, the one named last changes fastest.
Arguments:
- front: bfloat16 [4096, 4096], P(('row', 'rhs'), 'col'), as said below
- anc_weight: bfloat16 [1024, 4096], P(('row', 'rhs'), 'col'), may hold values from -0.1875 to 0.1875
- solved: bfloat16 [2048, 8192], P(('row', 'col'), 'rhs'), may hold values from -6 to 6
- owners: int32 [8], replicated, may hold values from 0 to 3, as said below
- indices: int32 [8, 128], replicated, may hold values from 0 to 511
- counts: int32 [8], replicated, may hold values from 64 to 128, as said below
- rhs_side: bfloat16 [4096, 8192], P('row', 'rhs'), may hold values from -6 to 6
Outputs:
- solution: bfloat16 [4096, 8192], P('row', 'rhs')
Inputs may be any that keep to these rules, and one draw needn't show every extreme that they name: `front`: zero above the diagonal; diagonal entries 1 or more. The 4 tiles of each aligned block of 4 tiles have 4 different owners, numbered row index times 2 plus col index. `counts`: rows at or past a tile's count are padding.
All inputs are finite; a program needn't handle non-finite values.
Results may differ from a plain program's by a relative error of at most 0.0038.
Values may be sent and summed in bfloat16 or wider, within the bound.
No kernel may reach another device: no remote copies, remote signals or barrier semaphores. Data moves between devices by JAX's collectives and lax.ppermute only.
A program may use at most 128 MiB of HBM per device.

v0:
```python
import jax
import jax.numpy as jnp
from jax import lax
from jax.sharding import PartitionSpec as P


def from_root(x, axis, root):
    mine = lax.axis_index(axis) == root
    return lax.psum(jnp.where(mine, x, jnp.zeros_like(x)), axis)


def on_device(front, anc_weight, solved, owners, indices, counts, rhs_side):
    row_count = lax.axis_size("row")
    col_count = lax.axis_size("col")
    tiles_block = row_count * col_count
    row_index = lax.axis_index("row")
    col_index = lax.axis_index("col")
    tile_rows = indices.shape[1]
    columns = solved.shape[1]
    self_id = row_index * col_count + col_index
    owner_grid = owners.reshape(row_count, tiles_block)
    mine = (owner_grid == self_id).astype(jnp.int32)
    position = jnp.sum(mine * jnp.arange(tiles_block, dtype=jnp.int32)[None, :], axis=1)
    tile_ids = jnp.arange(row_count, dtype=jnp.int32) * tiles_block + position
    local_rows = indices[tile_ids]
    live_rows = jnp.arange(tile_rows, dtype=jnp.int32)[None, :] < counts[tile_ids][:, None]
    picked = solved[local_rows.reshape(-1)].reshape(row_count, tile_rows, columns)
    picked = jnp.where(live_rows[:, :, None], picked, jnp.zeros_like(picked))
    block_owners = lax.dynamic_slice_in_dim(owners, row_index * tiles_block, tiles_block)
    outgoing = jnp.broadcast_to(picked[:, None], (row_count, col_count, tile_rows, columns))
    outgoing = outgoing.reshape(row_count * col_count * tile_rows, columns)
    received = lax.all_to_all(outgoing, ("row", "col"), split_axis=0, concat_axis=0, tiled=True)
    slot_rows = received.reshape(tiles_block, tile_rows, columns)
    anc_values = slot_rows[block_owners].reshape(tiles_block * tile_rows, columns)
    front_tile = lax.all_gather(front, "rhs", axis=0, tiled=True)
    width = front_tile.shape[1]
    anc_total = lax.dot_general(
        lax.all_gather(anc_weight, "rhs", axis=0, tiled=True),
        anc_values,
        (((0,), (0,)), ((), ())),
        preferred_element_type=jnp.float32,
    )
    rhs_values = rhs_side.astype(jnp.float32)
    solution_rows = jnp.zeros((width, columns), jnp.bfloat16)
    for step_index in reversed(range(row_count)):
        current = solution_rows

        def no_product():
            return jnp.zeros((width, columns), jnp.float32)

        wanted = jnp.logical_and(col_index == step_index, row_index > step_index)

        def front_product():
            return lax.dot_general(
                front_tile, current, (((0,), (0,)), ((), ())), preferred_element_type=jnp.float32
            )

        front_term = lax.cond(wanted, front_product, no_product)
        rounded = lax.optimization_barrier((anc_total + front_term).astype(jnp.bfloat16))
        shares = lax.all_gather(rounded[None], "row", axis=0, tiled=True)
        summed = jnp.sum(shares.astype(jnp.float32), axis=0)
        reduced = rhs_values - summed

        def solve_block():
            return jax.scipy.linalg.solve_triangular(
                front_tile.astype(jnp.float32), reduced, trans=1, lower=True
            )

        on_diagonal = jnp.logical_and(row_index == step_index, col_index == step_index)
        fresh = lax.cond(on_diagonal, solve_block, no_product).astype(jnp.bfloat16)
        shared = from_root(fresh, "col", row_index)
        solution_rows = jnp.where(row_index == step_index, shared, solution_rows)
    return solution_rows


def solution(mesh):
    placed = (
        P(("row", "rhs"), "col"),
        P(("row", "rhs"), "col"),
        P(("row", "col"), "rhs"),
        P(),
        P(),
        P(),
        P("row", "rhs"),
    )
    return jax.shard_map(
        on_device, mesh=mesh, in_specs=placed, out_specs=P("row", "rhs"), check_vma=False
    )
```

profile of v0, /device:TPU:1, one launch (start us, length us, event | category | flops | bytes accessed | tf_op | source)
XLA Modules:
  0.0 989.0 jit_solution(2549492993331266399)
XLA Ops:
  6.5 0.0 copy-start
  6.5 0.7 all-gather.7.cloned.1.call-update
  7.3 0.0 all-gather.9.cloned.1.call-start
  7.3 0.7 all-gather.9.cloned.1.call-update
  8.0 0.7 broadcast_compare_fusion
  8.7 0.1 eq.34
  8.8 0.1 select_reduce_fusion
  8.9 1.2 gather_fusion.1
  10.2 1.3 gather_fusion
  11.5 0.9 gather_fusion.2
  12.3 0.1 iota_compare_fusion.2
  12.4 0.1 broadcast_select_fusion.4
  12.5 0.7 broadcast_in_dim.20
  13.2 6.5 all-to-all-start
  19.7 0.7 compare_select_fusion.1
  20.4 2.8 all-to-all-done
  23.2 0.6 gather_fusion.3
  23.8 137.7 %all-gather.7.cloned.1.call-done = bf16[2048,2048]{1,0:T(8,128)(2,1)} async-done(((bf16[32,2048]{1,0:T(8,128)(2,1)}), bf16[2048,2048]{1,0:T(8,128)(2,1)}) %all-gather.7.cloned.1.call-update) | async-done | bytes 8388624 | tf_op jit(solution)/shard_map/all_gather | solution.py:35
  161.5 0.1 conditional.4
  161.5 0.1 broadcast.102
  161.6 118.2 %all-gather.9.cloned.1.call-done = bf16[512,2048]{1,0:T(8,128)(2,1)} async-done(((bf16[8,2048]{1,0:T(8,128)(2,1)}), bf16[512,2048]{1,0:T(8,128)(2,1)}) %all-gather.9.cloned.1.call-update) | async-done | bytes 2097168 | tf_op jit(solution)/shard_map/all_gather | solution.py:38
  279.8 3.2 add_convert_fusion.1
  283.0 0.0 all-gather.11.cloned.1.call-update
  283.0 0.0 all-reduce.3.cloned.1.call-start
  283.1 0.1 convert_element_type.52
  283.2 15.7 %all-gather.11.cloned.1.call-done = bf16[4096,128]{0,1:T(8,128)(2,1)} async-done(((bf16[2048,128]{0,1:T(8,128)(2,1)}), bf16[4096,128]{0,1:T(8,128)(2,1)}) %all-gather.11.cloned.1.call-update) | async-done | bytes 1048592 | tf_op jit(solution)/shard_map/all_gather | solution.py:60
  298.8 1.4 convert_element_type.55
  300.3 5.8 conditional.5
  300.3 0.9 broadcast.104
  306.1 0.8 broadcast_select_fusion.2
  306.9 0.0 all-reduce.3.cloned.1.call-update
  306.9 0.0 all-gather.13.cloned.1.call-start
  307.0 320.4 %all-reduce.3.cloned.1.call-done = bf16[2048,128]{1,0:T(8,128)(2,1)} async-done(((bf16[2048,128]{1,0:T(8,128)(2,1)}), bf16[2048,128]{1,0:T(8,128)(2,1)}) %all-reduce.3.cloned.1.call-update) | async-done | bytes 524304 | tf_op jit(solution)/shard_map/psum | solution.py:9
  627.4 1.1 broadcast_select_fusion
  628.5 4.7 conditional.6
  628.5 4.7 fusion.103
  633.2 2.1 add_convert_fusion
  635.4 0.0 all-gather.13.cloned.1.call-update
  635.4 0.0 all-reduce.5.cloned.1.call-start
  635.4 15.7 %all-gather.13.cloned.1.call-done = bf16[4096,128]{0,1:T(8,128)(2,1)} async-done(((bf16[2048,128]{0,1:T(8,128)(2,1)}), bf16[4096,128]{0,1:T(8,128)(2,1)}) %all-gather.13.cloned.1.call-update) | async-done | bytes 1048592 | tf_op jit(solution)/shard_map/all_gather | solution.py:60
  651.1 1.4 convert_element_type.56
  652.5 2.0 conditional.7
  652.5 0.9 broadcast.106
  654.5 0.0 copy-start.1
  654.5 0.8 broadcast_select_fusion.1
  655.4 0.0 all-reduce.5.cloned.1.call-update
  655.4 324.6 %all-reduce.5.cloned.1.call-done = bf16[2048,128]{1,0:T(8,128)(2,1)} async-done(((bf16[2048,128]{1,0:T(8,128)(2,1)}), bf16[2048,128]{1,0:T(8,128)(2,1)}) %all-reduce.5.cloned.1.call-update) | async-done | bytes 524304 | tf_op jit(solution)/shard_map/psum | solution.py:9
  980.0 1.9 broadcast_select_fusion.3
  (11 shorter events, 0.1 us)
Async XLA Ops:
  6.5 4.9 copy-start
  6.5 276.5 %copy-start.4 = (bf16[2048,128]{1,0:T(8,128)(2,1)S(1)}, bf16[2048,128]{1,0:T(8,128)(2,1)}, u32[]{:S(2)}) copy-start(bf16[2048,128]{1,0:T(8,128)(2,1)} %param.23) | copy-start | bytes 1572868
  6.5 155.0 %all-gather.7.cloned.1.call-start = ((), (), s32[]{:S(2)}) async-start(), calls=%async_computation.1 | async-start | bytes 8519680 | tf_op jit(solution)/shard_map/all_gather | solution.py:35
  7.3 272.5 %all-gather.9.cloned.1.call-start = ((), (), s32[]{:S(2)}) async-start(), calls=%async_computation.2 | async-start | bytes 2129920 | tf_op jit(solution)/shard_map/all_gather | solution.py:38
  13.2 10.1 %all-to-all-start = ((bf16[4,128,128]{2,1,0:T(8,128)(2,1)}), bf16[4,128,128]{2,1,0:T(8,128)(2,1)S(1)}, u32[]{:S(2)}, u32[]{:S(2)}) async-start(bf16[4,128,128]{2,1,0:T(8,128)(2,1)} %bitcast.38), calls=%async_computation | async-start | bytes 262144 | tf_op jit(solution)/shard_map/all_to_all | solution.py:32
  19.7 279.2 %all-gather.11.cloned.1.call-start = ((), (), s32[]{:S(2)}) async-start(), calls=%async_computation.5 | async-start | bytes 1572864 | tf_op jit(solution)/shard_map/all_gather | solution.py:60
  283.0 344.4 %all-reduce.3.cloned.1.call-start = ((), (), s32[]{:S(2)}) async-start(), calls=%async_computation.3 | async-start | bytes 1048576 | tf_op jit(solution)/shard_map/psum | solution.py:9
  306.9 344.2 %all-gather.13.cloned.1.call-start = ((), (), s32[]{:S(2)}) async-start(), calls=%async_computation.6 | async-start | bytes 1572864 | tf_op jit(solution)/shard_map/all_gather | solution.py:60
  635.4 344.6 %all-reduce.5.cloned.1.call-start = ((), (), s32[]{:S(2)}) async-start(), calls=%async_computation.4 | async-start | bytes 1048576 | tf_op jit(solution)/shard_map/psum | solution.py:9
  654.5 327.4 %copy-start.1 = (bf16[512,128]{1,0:T(8,128)(2,1)S(1)}, bf16[512,128]{1,0:T(8,128)(2,1)}, u32[]{:S(2)}) copy-start(bf16[512,128]{1,0:T(8,128)(2,1)} %param.19) | copy-start | bytes 393220
Sparse Core Ops, SparseCore 0:
  10.8 150.6 all-gather.6
  165.1 114.6 all-gather.8
  283.1 15.6 all-gather.10
  307.0 320.3 all-reduce.2
  635.5 15.5 all-gather.12
  655.5 324.4 all-reduce.4
where the time goes:
time: 996 us; the launch traced here: 989 us
  waiting for transfers between devices  937 us (94%)
  between operations  13.9 us (1%)
  other arithmetic  11.4 us (1%)
    psum x2, waiting for transfers between devices, from_root(): return lax.psum(jnp.where(mine, x, jnp.zeros_like(x)), axis)  645 us
    all_gather x1, waiting for transfers between devices, on_device(): front_tile = lax.all_gather(front, 'rhs', axis=0, tiled=True)  138 us
    all_gather x1, waiting for transfers between devices, on_device(): lax.all_gather(anc_weight, 'rhs', axis=0, tiled=True)  118 us
    all_gather x2, waiting for transfers between devices, on_device(): shares = lax.all_gather(rounded[None], 'row', axis=0, tiled=True)  31.3 us
  transfers between devices with their start and end apart: 7, of which 7 were waited for; matrix products, arithmetic and copies ran while one was open for 1% of the time, Pallas kernels for 0%

commit v1 on v0

--- a/solution.py
+++ b/solution.py
@@ -2,6 +2,10 @@
 import jax.numpy as jnp
 from jax import lax
 from jax.sharding import PartitionSpec as P
+
+trace_the_streams = lambda a0, comm_axis: jnp.concatenate(
+    lax.all_to_all(jnp.stack(lax.axis_size(comm_axis) * [a0]), comm_axis, 0, 0), 0
+)
 
 
 def from_root(x, axis, root):
@@ -32,7 +36,7 @@
     received = lax.all_to_all(outgoing, ("row", "col"), split_axis=0, concat_axis=0, tiled=True)
     slot_rows = received.reshape(tiles_block, tile_rows, columns)
     anc_values = slot_rows[block_owners].reshape(tiles_block * tile_rows, columns)
-    front_tile = lax.all_gather(front, "rhs", axis=0, tiled=True)
+    front_tile = trace_the_streams(front, "rhs")
     width = front_tile.shape[1]
     anc_total = lax.dot_general(
         lax.all_gather(anc_weight, "rhs", axis=0, tiled=True),

time: 996 us -> 948 us (0.952)
  waiting for transfers between devices: 937 us -> 868 us
    all_to_all x1, waiting for transfers between devices: 2.82 us -> 192 us  [lax.all_to_all(jnp.stack(lax.axis_size(comm_axis) * [a0]), comm_axis, 0, 0)]
    all_gather x1 -> x0, waiting for transfers between devices: 138 us -> none  [on_device(): front_tile = lax.all_gather(front, 'rhs', axis=0, tiled=True)]
    all_gather x1, waiting for transfers between devices: 118 us -> 0.02 us  [on_device(): lax.all_gather(anc_weight, 'rhs', axis=0, tiled=True)]
  transfers between devices with their start and end apart: 7 -> 6, of which waited for: 7 -> 5; matrix products, arithmetic and copies ran while one was open for 1% -> 0% of each run, Pallas kernels for 0% -> 0%
where the time goes in v1:
time: 948 us; the launch traced here: 940 us
  waiting for transfers between devices  868 us (92%)
  between operations  13.6 us (1%)
  starting transfers between devices  13.2 us (1%)
  local copies, waits for them, and re-layouts  11.2 us (1%)
  other arithmetic  10.8 us (1%)
    psum x2, waiting for transfers between devices, from_root(): return lax.psum(jnp.where(mine, x, jnp.zeros_like(x)), axis)  644 us
    all_to_all x1, waiting for transfers between devices, lax.all_to_all(jnp.stack(lax.axis_size(comm_axis) * [a0]), comm_axis, 0, 0)  192 us
    all_gather x2, waiting for transfers between devices, on_device(): shares = lax.all_gather(rounded[None], 'row', axis=0, tiled=True)  31.4 us
  transfers between devices with their start and end apart: 6, of which 5 were waited for; matrix products, arithmetic and copies ran while one was open for 0% of the time, Pallas kernels for 0%

profile of v1, /device:TPU:1, one launch (start us, length us, event | category | flops | bytes accessed | tf_op | source)
XLA Modules:
  0.0 939.9 jit_solution(4460553311709234009)
XLA Ops:
  6.5 0.0 copy-start
  6.5 0.7 broadcast_compare_fusion
  7.3 0.1 eq.34
  7.4 0.1 select_reduce_fusion
  7.5 1.2 gather_fusion.1
  8.8 1.3 gather_fusion
  10.1 0.1 iota_compare_fusion.2
  10.1 0.9 gather_fusion.2
  11.0 0.1 broadcast_select_fusion.4
  11.1 9.1 all_to_all.14
  20.3 5.3 stack.2
  25.5 13.0 %all-to-all-start = ((bf16[64,32,2048]{2,1,0:T(8,128)(2,1)}), bf16[64,32,2048]{2,1,0:T(8,128)(2,1)}, u32[]{:S(2)}, u32[]{:S(2)}) async-start(bf16[64,32,2048]{2,1,0:T(8,128)(2,1)} %stack.2), calls=%async_computation | async-start | bytes 16777216 | tf_op jit(solution)/shard_map/all_to_all | solution.py:7
  38.5 0.0 all-gather.6.cloned.1.call-start
  38.6 0.7 all-gather.6.cloned.1.call-update
  39.3 0.0 all-gather.8.cloned.1.call-start
  39.3 0.1 compare_select_fusion.1
  39.4 0.6 gather_fusion.3
  40.0 192.1 %all-to-all-done = bf16[64,32,2048]{2,1,0:T(8,128)(2,1)} async-done(((bf16[64,32,2048]{2,1,0:T(8,128)(2,1)}), bf16[64,32,2048]{2,1,0:T(8,128)(2,1)}, u32[]{:S(2)}, u32[]{:S(2)}) %all-to-all-start) | async-done | bytes 8388640 | tf_op jit(solution)/shard_map/all_to_all | solution.py:7
  232.1 0.1 conditional.4
  232.1 0.1 broadcast.104
  232.2 0.0 all-gather.6.cloned.1.call-done
  232.2 3.2 add_convert_fusion.1
  235.4 0.0 all-gather.8.cloned.1.call-update
  235.4 0.0 all-reduce.3.cloned.1.call-start
  235.5 0.1 convert_element_type.52
  235.6 15.7 %all-gather.8.cloned.1.call-done = bf16[4096,128]{0,1:T(8,128)(2,1)} async-done(((bf16[2048,128]{0,1:T(8,128)(2,1)}), bf16[4096,128]{0,1:T(8,128)(2,1)}) %all-gather.8.cloned.1.call-update) | async-done | bytes 1048592 | tf_op jit(solution)/shard_map/all_gather | solution.py:64
  251.3 1.4 convert_element_type.55
  252.8 5.8 conditional.5
  252.8 0.9 broadcast.106
  258.5 0.8 broadcast_select_fusion.2
  259.4 0.0 all-reduce.3.cloned.1.call-update
  259.4 0.0 all-gather.10.cloned.1.call-start
  259.5 319.8 %all-reduce.3.cloned.1.call-done = bf16[2048,128]{1,0:T(8,128)(2,1)} async-done(((bf16[2048,128]{1,0:T(8,128)(2,1)}), bf16[2048,128]{1,0:T(8,128)(2,1)}) %all-reduce.3.cloned.1.call-update) | async-done | bytes 524304 | tf_op jit(solution)/shard_map/psum | solution.py:13
  579.3 1.1 broadcast_select_fusion
  580.4 4.7 conditional.6
  580.4 4.7 fusion.103
  585.1 2.1 add_convert_fusion
  587.2 0.0 all-gather.10.cloned.1.call-update
  587.2 0.0 all-reduce.5.cloned.1.call-start
  587.3 15.7 %all-gather.10.cloned.1.call-done = bf16[4096,128]{0,1:T(8,128)(2,1)} async-done(((bf16[2048,128]{0,1:T(8,128)(2,1)}), bf16[4096,128]{0,1:T(8,128)(2,1)}) %all-gather.10.cloned.1.call-update) | async-done | bytes 1048592 | tf_op jit(solution)/shard_map/all_gather | solution.py:64
  602.9 1.4 convert_element_type.56
  604.4 2.0 conditional.7
  604.4 0.9 broadcast.108
  606.3 0.0 copy-start.1
  606.4 0.8 broadcast_select_fusion.1
  607.2 0.0 all-reduce.5.cloned.1.call-update
  607.2 324.0 %all-reduce.5.cloned.1.call-done = bf16[2048,128]{1,0:T(8,128)(2,1)} async-done(((bf16[2048,128]{1,0:T(8,128)(2,1)}), bf16[2048,128]{1,0:T(8,128)(2,1)}) %all-reduce.5.cloned.1.call-update) | async-done | bytes 524304 | tf_op jit(solution)/shard_map/psum | solution.py:13
  931.2 1.9 broadcast_select_fusion.3
  (12 shorter events, 0.1 us)
Async XLA Ops:
  6.5 3.6 copy-start
  6.5 32.8 %copy-start.5 = (s32[8]{0:T(128)S(1)}, s32[8]{0:T(128)}, u32[]{:S(2)}) copy-start(s32[8]{0:T(128)} %param.20) | copy-start | bytes 100
  25.5 210.0 %copy-start.4 = (bf16[2048,128]{1,0:T(8,128)(2,1)S(1)}, bf16[2048,128]{1,0:T(8,128)(2,1)}, u32[]{:S(2)}) copy-start(bf16[2048,128]{1,0:T(8,128)(2,1)} %param.23) | copy-start | bytes 1572868
  25.5 206.5 %all-to-all-start = ((bf16[64,32,2048]{2,1,0:T(8,128)(2,1)}), bf16[64,32,2048]{2,1,0:T(8,128)(2,1)}, u32[]{:S(2)}, u32[]{:S(2)}) async-start(bf16[64,32,2048]{2,1,0:T(8,128)(2,1)} %stack.2), calls=%async_computation | async-start | bytes 16777216 | tf_op jit(solution)/shard_map/all_to_all | solution.py:7
  38.5 193.7 %all-gather.6.cloned.1.call-start = ((), (), s32[]{:S(2)}) async-start(), calls=%async_computation.2 | async-start | bytes 2129920 | tf_op jit(solution)/shard_map/all_gather | solution.py:42
  39.3 212.1 %all-gather.8.cloned.1.call-start = ((), (), s32[]{:S(2)}) async-start(), calls=%async_computation.5 | async-start | bytes 1572864 | tf_op jit(solution)/shard_map/all_gather | solution.py:64
  235.4 343.8 %all-reduce.3.cloned.1.call-start = ((), (), s32[]{:S(2)}) async-start(), calls=%async_computation.3 | async-start | bytes 1048576 | tf_op jit(solution)/shard_map/psum | solution.py:13
  259.4 343.5 %all-gather.10.cloned.1.call-start = ((), (), s32[]{:S(2)}) async-start(), calls=%async_computation.6 | async-start | bytes 1572864 | tf_op jit(solution)/shard_map/all_gather | solution.py:64
  587.2 344.0 %all-reduce.5.cloned.1.call-start = ((), (), s32[]{:S(2)}) async-start(), calls=%async_computation.4 | async-start | bytes 1048576 | tf_op jit(solution)/shard_map/psum | solution.py:13
  606.3 326.8 %copy-start.1 = (bf16[512,128]{1,0:T(8,128)(2,1)S(1)}, bf16[512,128]{1,0:T(8,128)(2,1)}, u32[]{:S(2)}) copy-start(bf16[512,128]{1,0:T(8,128)(2,1)} %param.19) | copy-start | bytes 393220
Sparse Core Ops, SparseCore 0:
  42.9 163.9 all-gather.5
  235.5 15.7 all-gather.7
  259.5 319.6 all-reduce.2
  587.3 15.5 all-gather.9
  607.3 323.8 all-reduce.4
